TPU v7x, 512 devices: a whole 4x4x16 slice. The times are simulated.
512 devices in a mesh: expert: 64 (over x_hi, z, core), dp: 8 (over x_lo, y).
Axes of the slice: x: 4 (x_hi: 2, x_lo: 2; x = x_hi * 2 + x_lo), y: 4, z: 16, core: 2. Of those that a mesh axis runs over, the one named last changes fastest.
Arguments:
- skip_stream: bfloat16 [4096, 4096], P(('expert', 'dp')), may hold values from -6 to 6
- attention_probes: bfloat16 [4096, 4096], P(('expert', 'dp')), may hold values from -5 to 5
- stored_attention_lookups: bfloat16 [4096, 16, 512], P(('expert', 'dp')), may hold values from -5 to 5
- stored_attention_contents: bfloat16 [4096, 16, 512], P(('expert', 'dp')), may hold values from -6 to 6
- incoming_lookup_entries: bfloat16 [4096, 512], P(('expert', 'dp')), may hold values from -6 to 6
- incoming_content_entries: bfloat16 [4096, 512], P(('expert', 'dp')), may hold values from -6 to 6
- filled_slot_spans: int32 [4096], P(('expert', 'dp')), may hold values from 2 to 16, as said below
- layernorm_gain: float32 [4096], replicated, may hold values from 0.1 to 1.9
- routed_specialist_indices: int32 [4096, 8], P(('expert', 'dp')), may hold values from 0 to 63, all different within a row; in each aligned block of 8 rows (0 to 7, 8 to 15, ...) at most 2 rows name the same one
- routing_probabilities: float32 [4096, 8], P(('expert', 'dp')), may hold values from 0.05 to 1
- admission_limits: int32 [64], replicated, may hold values from 256 to 1024
- swap_indicator: int32 [64], replicated, may hold values from 0 to 1, as said below
- gating_projection_matrix: bfloat16 [64, 768, 4096], P('expert', 'dp'), may hold values from -0.09375 to 0.09375
- widening_projection_matrix: bfloat16 [64, 768, 4096], P('expert', 'dp'), may hold values from -0.09375 to 0.09375
- output_projection_matrix: bfloat16 [64, 768, 4096], P('expert', None, 'dp'), may hold values from -0.21875 to 0.21875
Outputs:
- layer_out: bfloat16 [4096, 4096], P(('expert', 'dp'))
- device_share: float32 [64], P('expert')
- held_gate: bfloat16 [64, 768, 4096], P('expert', 'dp')
- held_up: bfloat16 [64, 768, 4096], P('expert', 'dp')
- held_down: bfloat16 [64, 768, 4096], P('expert', None, 'dp')
Inputs may be any that keep to these rules, and one draw needn't show every extreme that they name: `filled_slot_spans`: each sequence has 2 or more valid slots and some sequence has all 16. `routed_specialist_indices`: in each aligned block of 8 rows (the rows of one device) no expert is named by more than 2 rows; the entries of a row differ. swap_indicator[i] equals swap_indicator[i + 32].
All inputs are finite; a program needn't handle non-finite values.
Results may differ from a plain program's by a relative error of at most 0.017.
Values may be sent and summed in bfloat16 or wider, within the bound.
No kernel may reach another device: no remote copies, remote signals or barrier semaphores. Data moves between devices by JAX's collectives and lax.ppermute only.
A program may use at most 64 MiB of HBM per device.

v0:
```python
import jax
import jax.numpy as jnp
from jax import lax
from jax.sharding import PartitionSpec as P

QH = 32
KVH = 4
HEAD = 128


def swapped(value, axis, stride):
    mask = 2**stride
    pairs = [(source, source ^ mask) for source in range(lax.axis_size(axis))]
    return lax.ppermute(value, axis, pairs)


def attention(query_rows, key_rows, value_rows, new_key, new_value, valid_len):
    seq_count = query_rows.shape[0]
    cache_len = key_rows.shape[1]
    group = QH // KVH
    scale = HEAD ** (-0.5)
    query_view = query_rows.reshape(seq_count, KVH, group, HEAD)
    key_view = key_rows.reshape(seq_count, cache_len, KVH, HEAD)
    value_view = value_rows.reshape(seq_count, cache_len, KVH, HEAD)
    scores = (
        jnp.einsum("skgd,slkd->skgl", query_view, key_view, preferred_element_type=jnp.float32)
        * scale
    )
    valid = lax.broadcasted_iota(jnp.int32, (seq_count, cache_len), 1) < valid_len[:, None]
    scores = jnp.where(valid[:, None, None, :], scores, -1e30)
    own_score = (
        jnp.einsum(
            "skgd,skd->skg",
            query_view,
            new_key.reshape(seq_count, KVH, HEAD),
            preferred_element_type=jnp.float32,
        )
        * scale
    )
    highest = jnp.maximum(jnp.max(scores, axis=-1), own_score)
    weights = jnp.exp(scores - highest[..., None])
    own_weight = jnp.exp(own_score - highest)
    denom = jnp.sum(weights, axis=-1) + own_weight
    probs = (weights / denom[..., None]).astype(jnp.bfloat16)
    own_prob = (own_weight / denom).astype(jnp.bfloat16)
    mixed = jnp.einsum("skgl,slkd->skgd", probs, value_view, preferred_element_type=jnp.float32)
    mixed = mixed + own_prob.astype(jnp.float32)[..., None] * new_value.reshape(
        seq_count, KVH, 1, HEAD
    ).astype(jnp.float32)
    return mixed.reshape(seq_count, QH * HEAD).astype(jnp.bfloat16)


def per_device(
    skip_stream,
    attention_probes,
    stored_attention_lookups,
    stored_attention_contents,
    incoming_lookup_entries,
    incoming_content_entries,
    filled_slot_spans,
    layernorm_gain,
    routed_specialist_indices,
    routing_probabilities,
    admission_limits,
    swap_indicator,
    gating_projection_matrix,
    widening_projection_matrix,
    output_projection_matrix,
):
    experts = lax.axis_size("expert")
    groups = lax.axis_size("dp")
    half_axis = experts // 2
    far_bit = experts.bit_length() - 2
    my_index = lax.axis_index("expert")
    my_device = my_index * groups + lax.axis_index("dp")
    own_weights = (
        gating_projection_matrix[0],
        widening_projection_matrix[0],
        output_projection_matrix[0],
    )
    partner = swapped(own_weights, "expert", far_bit)
    take_other = swap_indicator[my_index] == 1
    gate_held = jnp.where(take_other, partner[0], own_weights[0])
    up_held = jnp.where(take_other, partner[1], own_weights[1])
    down_held = jnp.where(take_other, partner[2], own_weights[2])
    retained_specialist = jnp.where(take_other, (my_index + half_axis) % experts, my_index)
    seq_rows = skip_stream.shape[0]
    top_count = routed_specialist_indices.shape[1]
    width = skip_stream.shape[1]
    slot_cap = 2
    expert_range = lax.broadcasted_iota(jnp.int32, (experts,), 0)
    all_routes = lax.all_gather(routed_specialist_indices, ("expert", "dp"), axis=0, tiled=True)
    all_hot = jnp.sum(
        (all_routes[:, :, None] == expert_range[None, None, :]).astype(jnp.int32), axis=1
    )
    all_rows = lax.broadcasted_iota(jnp.int32, (all_routes.shape[0], 1), 0)
    before_mine = jnp.sum(jnp.where(all_rows < my_device * seq_rows, all_hot, 0), axis=0)
    tallies = jnp.sum(all_hot, axis=0)
    route_hot = (routed_specialist_indices[:, :, None] == expert_range[None, None, :]).astype(
        jnp.int32
    )
    row_hot = jnp.sum(route_hot, axis=1)
    earlier = jnp.cumsum(row_hot, axis=0) - row_hot
    local_rank = jnp.sum(route_hot * earlier[:, None, :], axis=-1)
    global_rank = local_rank + jnp.sum(route_hot * before_mine[None, None, :], axis=-1)
    pair_limit = jnp.sum(route_hot * admission_limits[None, None, :], axis=-1)
    kept = global_rank < pair_limit
    held_tally = jnp.sum(jnp.where(expert_range == retained_specialist, tallies, 0))
    device_share = jnp.minimum(held_tally, admission_limits[retained_specialist]).astype(
        jnp.float32
    ) / (seq_rows * top_count * groups)
    attn = attention(
        attention_probes,
        stored_attention_lookups,
        stored_attention_contents,
        incoming_lookup_entries,
        incoming_content_entries,
        filled_slot_spans,
    )
    stream = skip_stream.astype(jnp.float32) + attn.astype(jnp.float32)
    normed = (
        stream
        * lax.rsqrt(jnp.mean(stream * stream, axis=-1, keepdims=True) + 1e-06)
        * layernorm_gain
    ).astype(jnp.bfloat16)
    slot_code = routed_specialist_indices * slot_cap + local_rank
    targets = lax.broadcasted_iota(jnp.int32, (experts * slot_cap,), 0)
    slot_hits = jnp.any(slot_code[:, :, None] == targets[None, None, :], axis=1)
    occupied = jnp.any(slot_hits, axis=0)
    row_range = lax.broadcasted_iota(jnp.int32, (seq_rows, 1), 0)
    source_row = jnp.sum(jnp.where(slot_hits, row_range, 0), axis=0) + jnp.where(
        occupied, 0, seq_rows
    )
    padded_rows = jnp.concatenate([normed, jnp.zeros((1, width), jnp.bfloat16)], axis=0)
    outgoing = padded_rows[source_row].reshape(experts, slot_cap, width)
    arrived_rows = lax.all_to_all(outgoing, "expert", split_axis=0, concat_axis=0, tiled=True)
    column_rows = lax.all_gather(arrived_rows, "dp", axis=1, tiled=True)
    gate_val = jnp.einsum(
        "esf,hf->esh", column_rows, own_weights[0], preferred_element_type=jnp.float32
    )
    up_val = jnp.einsum(
        "esf,hf->esh", column_rows, own_weights[1], preferred_element_type=jnp.float32
    )
    hidden = (jax.nn.silu(gate_val) * up_val).astype(jnp.bfloat16)
    feature_cols = own_weights[2].shape[1]
    summed = jnp.einsum(
        "esn,nf->esf",
        lax.all_gather(hidden, "dp", axis=2, tiled=True),
        own_weights[2],
        preferred_element_type=jnp.float32,
    )
    results = summed.astype(jnp.bfloat16).reshape(experts, groups, slot_cap, feature_cols)
    returned = lax.all_to_all(
        lax.all_to_all(results, "expert", split_axis=0, concat_axis=0, tiled=True),
        "dp",
        split_axis=1,
        concat_axis=3,
        tiled=True,
    )
    returned_flat = returned.reshape(experts * slot_cap, width)
    picked = returned_flat[slot_code]
    factor = jnp.where(kept, routing_probabilities, 0.0)
    expert_mix = jnp.sum(factor[:, :, None] * picked.astype(jnp.float32), axis=1)
    layer_out = (stream + expert_mix).astype(jnp.bfloat16)
    return (layer_out, device_share.reshape(1), gate_held[None], up_held[None], down_held[None])


def solution(mesh):
    in_specs = (
        P(("expert", "dp"), None),
        P(("expert", "dp"), None),
        P(("expert", "dp"), None, None),
        P(("expert", "dp"), None, None),
        P(("expert", "dp"), None),
        P(("expert", "dp"), None),
        P(("expert", "dp")),
        P(),
        P(("expert", "dp"), None),
        P(("expert", "dp"), None),
        P(),
        P(),
        P("expert", "dp", None),
        P("expert", "dp", None),
        P("expert", None, "dp"),
    )
    out_specs = (
        P(("expert", "dp"), None),
        P("expert"),
        P("expert", "dp", None),
        P("expert", "dp", None),
        P("expert", None, "dp"),
    )
    return jax.shard_map(
        per_device, mesh=mesh, in_specs=in_specs, out_specs=out_specs, check_vma=False
    )
```

profile of v0, /device:TPU:1, one launch (start us, length us, event | category | flops | bytes accessed | tf_op | source)
XLA Modules:
  0.0 1606.2 jit_solution(4724986277860716594)
XLA Ops:
  7.2 0.0 copy-start
  7.2 0.0 copy-start.4
  7.2 0.0 copy-start.3
  7.2 0.0 copy-start.7
  7.2 0.0 copy-start.5
  7.2 0.0 all-gather.3.cloned.1.call-start
  7.3 1247.2 %all_gather.9 = s32[4096,8]{1,0:T(8,128)S(1)} all-gather(s32[8,8]{1,0:T(8,128)} %param.23), channel_id=1, replica_groups=mesh['expert'=64,'dp'=8] {'expert','dp'}, dimensions={0}, use_global_device_ids=true | all-gather | bytes 131328 | tf_op jit(solution)/shard_map/all_gather | solution.py:92
  1254.5 0.8 convert_reduce_fusion.2
  1255.3 0.7 iota_compare_fusion.4
  1256.0 1.0 fusion.17
  1257.0 1.2 fusion.28
  1258.2 0.2 fusion.14
  1258.5 0.7 bitcast_convert_fusion
  1259.2 0.3 fusion.4
  1259.5 1.0 multiply_reduce_fusion
  1260.5 0.6 copy.48
  1261.1 1.9 convert_reduce_fusion
  1263.0 0.2 select_reduce_fusion
  1263.2 0.0 copy-done.4
  1263.2 0.0 copy-done.7
  1263.2 0.5 select_reduce_fusion.2
  1263.7 0.1 fusion.20
  1263.9 0.1 multiply_convert_fusion
  1264.0 0.0 copy-start.2
  1264.0 1.2 gather_fusion
  1265.2 0.7 reshape.129
  1266.0 72.0 %all_to_all.25 = bf16[64,2,4096]{2,1,0:T(2,128)(2,1)S(1)} all-to-all(bf16[64,2,4096]{2,1,0:T(2,128)(2,1)S(1)} %reshape.129), channel_id=1, replica_groups=mesh['expert'=64,'dp'=8] {'expert'}, dimensions={0} | all-to-all | bytes 2097152 | tf_op jit(solution)/shard_map/all_to_all | solution.py:136
  1338.0 1.7 copy.49
  1339.7 0.0 all-gather.3.cloned.1.call-update
  1339.7 0.2 all-gather.5.cloned.1.call-start
  1339.9 92.2 %all-gather.3.cloned.1.call-done = bf16[64,16,4096]{2,0,1:T(8,128)(2,1)} async-done(((bf16[64,2,4096]{2,0,1:T(8,128)(2,1)}), bf16[64,16,4096]{2,0,1:T(8,128)(2,1)}) %all-gather.3.cloned.1.call-update) | async-done | bytes 8388624 | tf_op jit(solution)/shard_map/all_gather | solution.py:137
  1432.1 5.8 fusion.8
  1438.0 2.4 fusion
  1440.4 0.0 copy-start.9
  1440.4 0.0 copy-start.6
  1440.4 1.1 copy.50
  1441.5 0.0 all-gather.5.cloned.1.call-update
  1441.5 48.3 %all-gather.5.cloned.1.call-done = bf16[64,16,768]{0,1,2:T(8,128)(2,1)} async-done(((bf16[64,16,96]{0,1,2:T(8,128)(2,1)}), bf16[64,16,768]{0,1,2:T(8,128)(2,1)}) %all-gather.5.cloned.1.call-update) | async-done | bytes 1572880 | tf_op jit(solution)/shard_map/all_gather | solution.py:148
  1489.8 5.5 copy.51
  1495.3 2.1 convolution_convert_fusion
  1497.4 1.2 reshape.130
  1498.7 18.1 %all-to-all-start.1 = ((bf16[64,8,2,512]{3,2,1,0:T(2,128)(2,1)}), bf16[64,8,2,512]{3,2,1,0:T(2,128)(2,1)S(1)}, u32[]{:S(2)}, u32[]{:S(2)}) async-start(bf16[64,8,2,512]{3,2,1,0:T(2,128)(2,1)} %reshape.130), calls=%async_computation.1 | async-start | bytes 2097152 | tf_op jit(solution)/shard_map/all_to_all | solution.py:154
  1516.7 4.9 collective-permute-start.2
  1521.7 1.9 collective-permute-start.1
  1523.6 4.9 collective-permute-start
  1528.5 0.6 dynamic_slice.6
  1529.7 0.1 reshape.145
  1529.8 0.6 dynamic_slice.7
  1530.4 0.6 fusion.26
  1532.4 10.7 collective-permute-done.2
  1543.1 2.1 select_bitcast_fusion
  1545.2 20.9 %collective-permute-done.1 = bf16[96,4096]{1,0:T(8,128)(2,1)S(1)} collective-permute-done((bf16[96,4096]{1,0:T(8,128)(2,1)}, bf16[96,4096]{1,0:T(8,128)(2,1)S(1)}, u32[]{:S(2)}, u32[]{:S(2)}) %collective-permute-start.1) | collective-permute-done | bytes 786464 | tf_op jit(solution)/shard_map/ppermute | solution.py:14
  1566.1 2.1 select_bitcast_fusion.1
  1568.2 0.4 all-to-all-done.1
  1568.6 1.8 copy.52
  1570.4 3.8 all-to-all-start.2
  1574.2 9.1 collective-permute-done
  1583.3 2.1 select_bitcast_fusion.2
  1585.4 9.3 all-to-all-done.2
  1594.7 1.1 copy.53
  1595.8 0.4 copy.59
  1596.2 0.9 gather_fusion.1
  1597.1 0.4 fusion.5
  1597.5 0.7 add_convert_fusion
  (24 shorter events, 0.2 us)
Async XLA Ops:
  7.2 1252.0 %copy-start = (bf16[8,16,512]{2,1,0:T(8,128)(2,1)S(1)}, bf16[8,16,512]{2,1,0:T(8,128)(2,1)}, u32[]{:S(2)}) copy-start(bf16[8,16,512]{2,1,0:T(8,128)(2,1)} %param.18) | copy-start | bytes 393220
  7.2 1256.0 %copy-start.4 = (s32[8,8]{1,0:T(8,128)S(1)}, s32[8,8]{1,0:T(8,128)}, u32[]{:S(2)}) copy-start(s32[8,8]{1,0:T(8,128)} %param.23) | copy-start | bytes 772
  7.2 1256.7 %copy-start.3 = (bf16[8,4096]{1,0:T(8,128)(2,1)S(1)}, bf16[8,4096]{1,0:T(8,128)(2,1)}, u32[]{:S(2)}) copy-start(bf16[8,4096]{1,0:T(8,128)(2,1)} %param.15) | copy-start | bytes 196612
  7.2 1256.0 %copy-start.7 = (s32[64]{0:T(128)S(1)}, s32[64]{0:T(128)}, u32[]{:S(2)}) copy-start(s32[64]{0:T(128)} %param.25) | copy-start | bytes 772
  7.2 1256.7 %copy-start.5 = (f32[4096]{0:T(1024)S(1)}, f32[4096]{0:T(1024)}, u32[]{:S(2)}) copy-start(f32[4096]{0:T(1024)} %param.22) | copy-start | bytes 49156
  7.2 1424.9 %all-gather.3.cloned.1.call-start = ((), (), s32[]{:S(2)}) async-start(), calls=%async_computation.3 | async-start | bytes 9437184 | tf_op jit(solution)/shard_map/all_gather | solution.py:137
  1264.0 168.1 %copy-start.2 = (bf16[1,96,4096]{2,1,0:T(8,128)(2,1)S(1)}, bf16[1,96,4096]{2,1,0:T(8,128)(2,1)}, u32[]{:S(2)}) copy-start(bf16[1,96,4096]{2,1,0:T(8,128)(2,1)} %param.27) | copy-start | bytes 2359300
  1339.7 98.3 %copy-start.1 = (bf16[1,96,4096]{2,1,0:T(8,128)(2,1)S(1)}, bf16[1,96,4096]{2,1,0:T(8,128)(2,1)}, u32[]{:S(2)}) copy-start(bf16[1,96,4096]{2,1,0:T(8,128)(2,1)} %param.28) | copy-start | bytes 2359300
  1339.7 150.1 %all-gather.5.cloned.1.call-start = ((), (), s32[]{:S(2)}) async-start(), calls=%async_computation.4 | async-start | bytes 3538944 | tf_op jit(solution)/shard_map/all_gather | solution.py:148
  1432.1 5.9 copy-start.8
  1440.4 88.1 %copy-start.9 = (s32[64]{0:T(128)S(1)}, s32[64]{0:T(128)}, u32[]{:S(2)}) copy-start(s32[64]{0:T(128)} %param.26) | copy-start | bytes 772
  1440.4 91.9 %copy-start.6 = (f32[8,8]{1,0:T(8,128)S(1)}, f32[8,8]{1,0:T(8,128)}, u32[]{:S(2)}) copy-start(f32[8,8]{1,0:T(8,128)} %param.24) | copy-start | bytes 772
  1498.7 69.9 %all-to-all-start.1 = ((bf16[64,8,2,512]{3,2,1,0:T(2,128)(2,1)}), bf16[64,8,2,512]{3,2,1,0:T(2,128)(2,1)S(1)}, u32[]{:S(2)}, u32[]{:S(2)}) async-start(bf16[64,8,2,512]{3,2,1,0:T(2,128)(2,1)} %reshape.130), calls=%async_computation.1 | async-start | bytes 2097152 | tf_op jit(solution)/shard_map/all_to_all | solution.py:154
  1516.7 26.4 %collective-permute-start.2 = (bf16[768,512]{1,0:T(8,128)(2,1)}, bf16[768,512]{1,0:T(8,128)(2,1)}, u32[]{:S(2)}, u32[]{:S(2)}) collective-permute-start(bf16[768,512]{1,0:T(8,128)(2,1)} %bitcast.80), channel_id=1, source_target_pairs={{0,256},{8,264},{16,272},{24,280},{32,288},{40,296},{48,304},{56,3... | collective-permute-start | bytes 2359304 | tf_op jit(solution)/shard_map/ppermute | solution.py:14
  1521.7 44.5 %collective-permute-start.1 = (bf16[96,4096]{1,0:T(8,128)(2,1)}, bf16[96,4096]{1,0:T(8,128)(2,1)S(1)}, u32[]{:S(2)}, u32[]{:S(2)}) collective-permute-start(bf16[96,4096]{1,0:T(8,128)(2,1)} %bitcast.81), channel_id=1, source_target_pairs={{0,256},{8,264},{16,272},{24,280},{32,288},{40,296},{48,304},{56,3... | collective-permute-start | bytes 2359304 | tf_op jit(solution)/shard_map/ppermute | solution.py:14
  1523.6 59.7 %collective-permute-start = (bf16[96,4096]{1,0:T(8,128)(2,1)}, bf16[96,4096]{1,0:T(8,128)(2,1)S(1)}, u32[]{:S(2)}, u32[]{:S(2)}) collective-permute-start(bf16[96,4096]{1,0:T(8,128)(2,1)} %bitcast.82), channel_id=1, source_target_pairs={{0,256},{8,264},{16,272},{24,280},{32,288},{40,296},{48,304},{56,3... | collective-permute-start | bytes 2359304 | tf_op jit(solution)/shard_map/ppermute | solution.py:14
  1570.4 24.3 %all-to-all-start.2 = ((bf16[64,8,2,512]{3,2,0,1:T(2,128)(2,1)}), bf16[64,8,2,512]{3,2,0,1:T(2,128)(2,1)S(1)}, u32[]{:S(2)}, u32[]{:S(2)}) async-start(bf16[64,8,2,512]{3,2,0,1:T(2,128)(2,1)} %copy.52), calls=%async_computation.2 | async-start | bytes 2097152 | tf_op jit(solution)/shard_map/all_to_all | solution.py:153
Sparse Core Ops, SparseCore 0:
  1339.8 92.2 all-gather.2
  1441.6 48.1 all-gather.4
where the time goes:
time: 1610 us
  blocking collectives  1320 us (82%)
  waiting for transfers between devices  191 us (12%)
  starting transfers between devices  33.8 us (2%)
  between operations  17.5 us (1%)
  local copies, waits for them, and re-layouts  17.4 us (1%)
    all_gather x1, blocking collectives, per_device(): lax.all_gather(routed_specialist_indices, ('expert', 'dp'), axis=0, tiled...  1250 us
    all_gather x1, waiting for transfers between devices, per_device(): column_rows = lax.all_gather(arrived_rows, 'dp', axis=1, tiled=True)  92.2 us
    all_to_all x1, blocking collectives, per_device(): lax.all_to_all(outgoing, 'expert', split_axis=0, concat_axis=0, tiled=True)  72 us
    all_gather x1, waiting for transfers between devices, per_device(): lax.all_gather(hidden, 'dp', axis=2, tiled=True)  48.3 us
    ppermute x3, waiting for transfers between devices, swapped(): return lax.ppermute(value, axis, pairs)  40.8 us
  transfers between devices with their start and end apart: 7, of which 7 were waited for; matrix products, arithmetic and copies ran while one was open for 1% of the time, Pallas kernels for 0%

commit v1 on v0

--- a/solution.py
+++ b/solution.py
@@ -89,7 +89,10 @@
     width = skip_stream.shape[1]
     slot_cap = 2
     expert_range = lax.broadcasted_iota(jnp.int32, (experts,), 0)
-    all_routes = lax.all_gather(routed_specialist_indices, ("expert", "dp"), axis=0, tiled=True)
+    devices = lax.axis_size(("expert", "dp"))
+    parts = jnp.stack([routed_specialist_indices for _ in range(devices)])
+    parts = lax.all_to_all(parts, ("expert", "dp"), split_axis=0, concat_axis=0)
+    all_routes = jnp.concatenate(parts, axis=0)
     all_hot = jnp.sum(
         (all_routes[:, :, None] == expert_range[None, None, :]).astype(jnp.int32), axis=1
     )

time: 1610 us -> 472 us (0.29)
  blocking collectives: 1320 us -> 56.9 us
  waiting for transfers between devices: 191 us -> 290 us
  starting transfers between devices: 33.8 us -> 58.1 us
    all_gather x1 -> x0, blocking collectives: 1250 us -> none  [per_device(): lax.all_gather(routed_specialist_indices, ('expert', 'dp'), axis=0, tiled...]
    all_to_all x0 -> x1, waiting for transfers between devices: none -> 97.8 us  [per_device(): parts = lax.all_to_all(parts, ('expert', 'dp'), split_axis=0, concat_axis=0)]
    all_to_all x0 -> x1, starting transfers between devices: none -> 24.3 us  [per_device(): parts = lax.all_to_all(parts, ('expert', 'dp'), split_axis=0, concat_axis=0)]
  transfers between devices with their start and end apart: 7 -> 8, of which waited for: 7 -> 8; matrix products, arithmetic and copies ran while one was open for 1% -> 3% of each run, Pallas kernels for 0% -> 0%
where the time goes in v1:
time: 472 us; the launch traced here: 471 us
  waiting for transfers between devices  290 us (61%)
  starting transfers between devices  58.1 us (12%)
  blocking collectives  56.9 us (12%)
  local copies, waits for them, and re-layouts  23.7 us (5%)
  between operations  17.5 us (4%)
  other arithmetic  12.9 us (3%)
  matrix products  12.8 us (3%)
    all_to_all x1, waiting for transfers between devices, per_device(): parts = lax.all_to_all(parts, ('expert', 'dp'), split_axis=0, concat_axis=0)  97.8 us
    all_gather x1, waiting for transfers between devices, per_device(): column_rows = lax.all_gather(arrived_rows, 'dp', axis=1, tiled=True)  92.9 us
    all_to_all x1, blocking collectives, per_device(): lax.all_to_all(outgoing, 'expert', split_axis=0, concat_axis=0, tiled=True)  56.9 us
    all_gather x1, waiting for transfers between devices, per_device(): lax.all_gather(hidden, 'dp', axis=2, tiled=True)  48.3 us
    ppermute x3, waiting for transfers between devices, swapped(): return lax.ppermute(value, axis, pairs)  40.8 us
    all_to_all x1, starting transfers between devices, per_device(): parts = lax.all_to_all(parts, ('expert', 'dp'), split_axis=0, concat_axis=0)  24.3 us
    all_to_all x1, starting transfers between devices, per_device(): lax.all_to_all(results, 'expert', split_axis=0, concat_axis=0, tiled=True)  18.1 us
    ppermute x3, starting transfers between devices, swapped(): return lax.ppermute(value, axis, pairs)  11.7 us
  transfers between devices with their start and end apart: 8, of which 8 were waited for; matrix products, arithmetic and copies ran while one was open for 3% of the time, Pallas kernels for 0%

profile of v1, /device:TPU:1, one launch (start us, length us, event | category | flops | bytes accessed | tf_op | source)
XLA Modules:
  0.0 471.4 jit_solution(12490455466653314028)
XLA Ops:
  7.2 0.0 copy-start
  7.2 0.0 copy-start.4
  7.2 0.0 copy-start.3
  7.2 0.8 copy.68
  8.0 1.5 stack.2
  9.5 24.3 %all-to-all-start = ((s32[512,8,8]{1,2,0:T(8,128)}), s32[512,8,8]{1,2,0:T(8,128)S(1)}, u32[]{:S(2)}, u32[]{:S(2)}) async-start(s32[512,8,8]{1,2,0:T(8,128)} %stack.2), calls=%async_computation | async-start | bytes 4194304 | tf_op jit(solution)/shard_map/all_to_all | solution.py:94
  33.8 0.0 all-gather.3.cloned.1.call-start
  33.9 0.7 iota_compare_fusion.4
  34.6 1.0 fusion.17
  35.6 1.2 fusion.28
  36.8 0.2 fusion.14
  37.1 0.7 bitcast_convert_fusion
  37.8 0.3 fusion.4
  38.1 0.2 multiply_reduce_fusion
  38.3 0.1 multiply_convert_fusion
  38.4 0.1 convert_reduce_fusion.2
  38.6 97.8 %all-to-all-done = s32[512,8,8]{1,2,0:T(8,128)S(1)} async-done(((s32[512,8,8]{1,2,0:T(8,128)}), s32[512,8,8]{1,2,0:T(8,128)S(1)}, u32[]{:S(2)}, u32[]{:S(2)}) %all-to-all-start) | async-done | bytes 131104 | tf_op jit(solution)/shard_map/all_to_all | solution.py:94
  136.3 1.7 copy.69
  138.1 2.8 eq.58
  140.9 1.9 convert_reduce_fusion
  142.7 0.2 select_reduce_fusion
  142.9 0.5 select_reduce_fusion.2
  143.5 0.1 fusion.20
  143.6 0.0 copy-start.2
  143.6 1.2 gather_fusion
  144.8 0.7 reshape.131
  145.5 56.9 %all_to_all.30 = bf16[64,2,4096]{2,1,0:T(2,128)(2,1)S(1)} all-to-all(bf16[64,2,4096]{2,1,0:T(2,128)(2,1)S(1)} %reshape.131), channel_id=1, replica_groups=mesh['expert'=64,'dp'=8] {'expert'}, dimensions={0} | all-to-all | bytes 2097152 | tf_op jit(solution)/shard_map/all_to_all | solution.py:139
  202.5 1.7 copy.70
  204.1 0.0 all-gather.3.cloned.1.call-update
  204.1 0.2 all-gather.5.cloned.1.call-start
  204.4 92.9 %all-gather.3.cloned.1.call-done = bf16[64,16,4096]{2,0,1:T(8,128)(2,1)} async-done(((bf16[64,2,4096]{2,0,1:T(8,128)(2,1)}), bf16[64,16,4096]{2,0,1:T(8,128)(2,1)}) %all-gather.3.cloned.1.call-update) | async-done | bytes 8388624 | tf_op jit(solution)/shard_map/all_gather | solution.py:140
  297.3 5.9 %fusion.8 = f32[64,16,96]{2,0,1:T(8,128)S(1)} fusion(bf16[64,16,4096]{2,0,1:T(8,128)(2,1)} %all-gather.3.cloned.1.call-done, bf16[1,96,4096]{2,1,0:T(8,128)(2,1)S(1)} %copy-done.2), kind=kOutput, calls=%fused_computation.19 | convolution fusion | flops 805306368 | bytes 9568256 | tf_op jit(solution)/shard_map/esf,hf->esh/dot_general | solution.py:141
  303.2 2.4 fusion
  305.6 0.0 copy-start.9
  305.6 0.0 copy-start.6
  305.6 1.1 copy.71
  306.7 0.0 all-gather.5.cloned.1.call-update
  306.7 48.3 %all-gather.5.cloned.1.call-done = bf16[64,16,768]{0,1,2:T(8,128)(2,1)} async-done(((bf16[64,16,96]{0,1,2:T(8,128)(2,1)}), bf16[64,16,768]{0,1,2:T(8,128)(2,1)}) %all-gather.5.cloned.1.call-update) | async-done | bytes 1572880 | tf_op jit(solution)/shard_map/all_gather | solution.py:151
  355.0 5.5 %copy.72 = bf16[64,16,768]{2,1,0:T(8,128)(2,1)S(1)} copy(bf16[64,16,768]{0,1,2:T(8,128)(2,1)} %all-gather.5.cloned.1.call-done) | data formatting | bytes 3145728 | tf_op jit(solution)/shard_map/all_gather | solution.py:151
  360.5 2.1 convolution_convert_fusion
  362.6 1.2 reshape.132
  363.9 18.1 %all-to-all-start.2 = ((bf16[64,8,2,512]{3,2,1,0:T(2,128)(2,1)}), bf16[64,8,2,512]{3,2,1,0:T(2,128)(2,1)S(1)}, u32[]{:S(2)}, u32[]{:S(2)}) async-start(bf16[64,8,2,512]{3,2,1,0:T(2,128)(2,1)} %reshape.132), calls=%async_computation.2 | async-start | bytes 2097152 | tf_op jit(solution)/shard_map/all_to_all | solution.py:157
  381.9 4.9 %collective-permute-start.2 = (bf16[768,512]{1,0:T(8,128)(2,1)}, bf16[768,512]{1,0:T(8,128)(2,1)}, u32[]{:S(2)}, u32[]{:S(2)}) collective-permute-start(bf16[768,512]{1,0:T(8,128)(2,1)} %bitcast.82), channel_id=1, source_target_pairs={{0,256},{8,264},{16,272},{24,280},{32,288},{40,296},{48,304},{56,3... | collective-permute-start | bytes 2359304 | tf_op jit(solution)/shard_map/ppermute | solution.py:14
  386.8 1.9 collective-permute-start.1
  388.8 4.9 %collective-permute-start = (bf16[96,4096]{1,0:T(8,128)(2,1)}, bf16[96,4096]{1,0:T(8,128)(2,1)S(1)}, u32[]{:S(2)}, u32[]{:S(2)}) collective-permute-start(bf16[96,4096]{1,0:T(8,128)(2,1)} %bitcast.84), channel_id=1, source_target_pairs={{0,256},{8,264},{16,272},{24,280},{32,288},{40,296},{48,304},{56,3... | collective-permute-start | bytes 2359304 | tf_op jit(solution)/shard_map/ppermute | solution.py:14
  393.7 0.6 dynamic_slice.6
  394.9 0.6 dynamic_slice.7
  395.5 0.1 reshape.147
  395.6 0.6 fusion.26
  397.6 10.7 %collective-permute-done.2 = bf16[768,512]{1,0:T(8,128)(2,1)} collective-permute-done((bf16[768,512]{1,0:T(8,128)(2,1)}, bf16[768,512]{1,0:T(8,128)(2,1)}, u32[]{:S(2)}, u32[]{:S(2)}) %collective-permute-start.2) | collective-permute-done | bytes 786464 | tf_op jit(solution)/shard_map/ppermute | solution.py:14
  408.3 2.1 select_bitcast_fusion
  410.4 20.9 %collective-permute-done.1 = bf16[96,4096]{1,0:T(8,128)(2,1)S(1)} collective-permute-done((bf16[96,4096]{1,0:T(8,128)(2,1)}, bf16[96,4096]{1,0:T(8,128)(2,1)S(1)}, u32[]{:S(2)}, u32[]{:S(2)}) %collective-permute-start.1) | collective-permute-done | bytes 786464 | tf_op jit(solution)/shard_map/ppermute | solution.py:14
  431.3 2.1 select_bitcast_fusion.1
  433.4 0.4 all-to-all-done.2
  433.8 1.8 copy.73
  435.6 3.8 all-to-all-start.3
  439.4 9.1 %collective-permute-done = bf16[96,4096]{1,0:T(8,128)(2,1)S(1)} collective-permute-done((bf16[96,4096]{1,0:T(8,128)(2,1)}, bf16[96,4096]{1,0:T(8,128)(2,1)S(1)}, u32[]{:S(2)}, u32[]{:S(2)}) %collective-permute-start) | collective-permute-done | bytes 786464 | tf_op jit(solution)/shard_map/ppermute | solution.py:14
  448.5 2.1 select_bitcast_fusion.2
  450.6 9.3 %all-to-all-done.3 = bf16[64,8,2,512]{3,2,0,1:T(2,128)(2,1)S(1)} async-done(((bf16[64,8,2,512]{3,2,0,1:T(2,128)(2,1)}), bf16[64,8,2,512]{3,2,0,1:T(2,128)(2,1)S(1)}, u32[]{:S(2)}, u32[]{:S(2)}) %all-to-all-start.3) | async-done | bytes 1048608 | tf_op jit(solution)/shard_map/all_to_all | solution.py:156
  459.9 1.1 copy.74
  461.0 0.4 copy.80
  461.4 0.9 gather_fusion.1
  462.3 0.4 fusion.5
  462.7 0.7 add_convert_fusion
  (28 shorter events, 0.2 us)
Async XLA Ops:
  7.2 30.6 %copy-start = (bf16[8,16,512]{2,1,0:T(8,128)(2,1)S(1)}, bf16[8,16,512]{2,1,0:T(8,128)(2,1)}, u32[]{:S(2)}) copy-start(bf16[8,16,512]{2,1,0:T(8,128)(2,1)} %param.18) | copy-start | bytes 393220
  7.2 31.2 %copy-start.4 = (s32[8,8]{1,0:T(8,128)S(1)}, s32[8,8]{1,0:T(8,128)}, u32[]{:S(2)}) copy-start(s32[8,8]{1,0:T(8,128)} %param.23) | copy-start | bytes 772
  7.2 30.9 %copy-start.3 = (bf16[8,4096]{1,0:T(8,128)(2,1)S(1)}, bf16[8,4096]{1,0:T(8,128)(2,1)}, u32[]{:S(2)}) copy-start(bf16[8,4096]{1,0:T(8,128)(2,1)} %param.15) | copy-start | bytes 196612
  7.2 31.1 %copy-start.5 = (f32[4096]{0:T(1024)S(1)}, f32[4096]{0:T(1024)}, u32[]{:S(2)}) copy-start(f32[4096]{0:T(1024)} %param.22) | copy-start | bytes 49156
  9.5 133.4 %copy-start.7 = (s32[64]{0:T(128)S(1)}, s32[64]{0:T(128)}, u32[]{:S(2)}) copy-start(s32[64]{0:T(128)} %param.25) | copy-start | bytes 772
  9.5 126.8 %all-to-all-start = ((s32[512,8,8]{1,2,0:T(8,128)}), s32[512,8,8]{1,2,0:T(8,128)S(1)}, u32[]{:S(2)}, u32[]{:S(2)}) async-start(s32[512,8,8]{1,2,0:T(8,128)} %stack.2), calls=%async_computation | async-start | bytes 4194304 | tf_op jit(solution)/shard_map/all_to_all | solution.py:94
  33.8 263.5 %all-gather.3.cloned.1.call-start = ((), (), s32[]{:S(2)}) async-start(), calls=%async_computation.4 | async-start | bytes 9437184 | tf_op jit(solution)/shard_map/all_gather | solution.py:140
  143.6 153.7 %copy-start.2 = (bf16[1,96,4096]{2,1,0:T(8,128)(2,1)S(1)}, bf16[1,96,4096]{2,1,0:T(8,128)(2,1)}, u32[]{:S(2)}) copy-start(bf16[1,96,4096]{2,1,0:T(8,128)(2,1)} %param.27) | copy-start | bytes 2359300
  204.1 99.1 %copy-start.1 = (bf16[1,96,4096]{2,1,0:T(8,128)(2,1)S(1)}, bf16[1,96,4096]{2,1,0:T(8,128)(2,1)}, u32[]{:S(2)}) copy-start(bf16[1,96,4096]{2,1,0:T(8,128)(2,1)} %param.28) | copy-start | bytes 2359300
  204.1 150.9 %all-gather.5.cloned.1.call-start = ((), (), s32[]{:S(2)}) async-start(), calls=%async_computation.5 | async-start | bytes 3538944 | tf_op jit(solution)/shard_map/all_gather | solution.py:151
  297.3 5.9 %copy-start.8 = (bf16[64,16,4096]{2,0,1:T(8,128)(2,1)S(1)}, bf16[64,16,4096]{2,0,1:T(8,128)(2,1)}, u32[]{:S(2)}) copy-start(bf16[64,16,4096]{2,0,1:T(8,128)(2,1)} %all-gather.3.cloned.1.call-done) | copy-start | bytes 25165828
  305.6 88.1 %copy-start.9 = (s32[64]{0:T(128)S(1)}, s32[64]{0:T(128)}, u32[]{:S(2)}) copy-start(s32[64]{0:T(128)} %param.26) | copy-start | bytes 772
  305.6 91.9 %copy-start.6 = (f32[8,8]{1,0:T(8,128)S(1)}, f32[8,8]{1,0:T(8,128)}, u32[]{:S(2)}) copy-start(f32[8,8]{1,0:T(8,128)} %param.24) | copy-start | bytes 772
  363.9 69.9 %all-to-all-start.2 = ((bf16[64,8,2,512]{3,2,1,0:T(2,128)(2,1)}), bf16[64,8,2,512]{3,2,1,0:T(2,128)(2,1)S(1)}, u32[]{:S(2)}, u32[]{:S(2)}) async-start(bf16[64,8,2,512]{3,2,1,0:T(2,128)(2,1)} %reshape.132), calls=%async_computation.2 | async-start | bytes 2097152 | tf_op jit(solution)/shard_map/all_to_all | solution.py:157
  381.9 26.4 %collective-permute-start.2 = (bf16[768,512]{1,0:T(8,128)(2,1)}, bf16[768,512]{1,0:T(8,128)(2,1)}, u32[]{:S(2)}, u32[]{:S(2)}) collective-permute-start(bf16[768,512]{1,0:T(8,128)(2,1)} %bitcast.82), channel_id=1, source_target_pairs={{0,256},{8,264},{16,272},{24,280},{32,288},{40,296},{48,304},{56,3... | collective-permute-start | bytes 2359304 | tf_op jit(solution)/shard_map/ppermute | solution.py:14
  386.8 44.5 %collective-permute-start.1 = (bf16[96,4096]{1,0:T(8,128)(2,1)}, bf16[96,4096]{1,0:T(8,128)(2,1)S(1)}, u32[]{:S(2)}, u32[]{:S(2)}) collective-permute-start(bf16[96,4096]{1,0:T(8,128)(2,1)} %bitcast.83), channel_id=1, source_target_pairs={{0,256},{8,264},{16,272},{24,280},{32,288},{40,296},{48,304},{56,3... | collective-permute-start | bytes 2359304 | tf_op jit(solution)/shard_map/ppermute | solution.py:14
  388.8 59.7 %collective-permute-start = (bf16[96,4096]{1,0:T(8,128)(2,1)}, bf16[96,4096]{1,0:T(8,128)(2,1)S(1)}, u32[]{:S(2)}, u32[]{:S(2)}) collective-permute-start(bf16[96,4096]{1,0:T(8,128)(2,1)} %bitcast.84), channel_id=1, source_target_pairs={{0,256},{8,264},{16,272},{24,280},{32,288},{40,296},{48,304},{56,3... | collective-permute-start | bytes 2359304 | tf_op jit(solution)/shard_map/ppermute | solution.py:14
  435.6 24.3 %all-to-all-start.3 = ((bf16[64,8,2,512]{3,2,0,1:T(2,128)(2,1)}), bf16[64,8,2,512]{3,2,0,1:T(2,128)(2,1)S(1)}, u32[]{:S(2)}, u32[]{:S(2)}) async-start(bf16[64,8,2,512]{3,2,0,1:T(2,128)(2,1)} %copy.73), calls=%async_computation.3 | async-start | bytes 2097152 | tf_op jit(solution)/shard_map/all_to_all | solution.py:156
Sparse Core Ops, SparseCore 0:
  204.3 93.0 all-gather.2
  306.8 48.1 all-gather.4
